TPU v7x, 32 devices: a whole 2x2x4 slice. The times are simulated.
32 devices in a mesh: owner: 2 (over x), reader: 16 (over z, y, core).
Axes of the slice: x: 2, y: 2, z: 4, core: 2. Of those that a mesh axis runs over, the one named last changes fastest.
Arguments:
- acts: bfloat16 [256, 4096], P('reader', 'owner'), may hold values from -6 to 6
- grads: bfloat16 [256, 14336], P('reader', 'owner'), may hold values from -6 to 6
- basis_a: bfloat16 [4096, 4096], P('reader', 'owner'), may hold values from -0.09375 to 0.09375
- basis_g: bfloat16 [14336, 14336], P('reader', 'owner'), may hold values from -0.046875 to 0.046875
- eigvals: bfloat16 [14336, 4096], P('reader', 'owner'), may hold values from 0.099609375 to 10
- lengths: int32 [2], replicated, may hold values from 1 to 128, as said below
- shuffle: int32 [2], replicated, may hold values from 0 to 1, each once
Outputs:
- token_score: float32 [256], P('owner')
- example_score: float32 [2], replicated
Inputs may be any that keep to these rules, and one draw needn't show every extreme that they name: `lengths`: some slot has exactly 128 live tokens. `shuffle`: each example id appears once.
All inputs are finite; a program needn't handle non-finite values.
Results may differ from a plain program's by a relative error of at most 0.0003.
Values may be sent and summed in bfloat16 or wider, within the bound.
No kernel may reach another device: no remote copies, remote signals or barrier semaphores. Data moves between devices by JAX's collectives and lax.ppermute only.
A program may use at most 128 MiB of HBM per device.

v0:
```python
import jax
import jax.numpy as jnp
from jax import lax
from jax.sharding import PartitionSpec as P

SEQ = 128


def local(acts, grads, basis_a, basis_g, eigvals, lengths, shuffle):
    owners = lax.axis_size("owner")
    readers = lax.axis_size("reader")
    owner_index = lax.axis_index("owner")
    rows = acts.shape[0] * readers
    slots = rows // SEQ
    m_block = basis_g.shape[0]
    n_block = basis_a.shape[0]
    width = eigvals.shape[1]
    dim_ff = m_block * readers
    dim_d = width * owners
    joined = jnp.concatenate([grads, acts], axis=1)
    joined = lax.all_gather(joined, "reader", axis=0, tiled=True)
    all_g = joined[:, : grads.shape[1]]
    all_a = joined[:, grads.shape[1] :]
    part_g = jnp.einsum("tk,jk->tj", all_g, basis_g, preferred_element_type=jnp.float32)
    part_a = jnp.einsum("tk,jk->tj", all_a, basis_a, preferred_element_type=jnp.float32)
    part = jnp.concatenate([part_g, part_a], axis=1)
    whole = lax.psum(part, "owner")
    token = jnp.arange(rows, dtype=jnp.int32)
    live = (token % SEQ < lengths[token // SEQ]).astype(jnp.float32)
    rot = (whole * live[:, None]).astype(jnp.bfloat16)
    rot_g = rot[:, :m_block]
    rot_a_block = rot[:, m_block:]
    rot_a_all = lax.all_gather(rot_a_block, "reader", axis=1, tiled=True)
    rot_a = lax.dynamic_slice_in_dim(rot_a_all, owner_index * width, width, axis=1)
    denom = eigvals.astype(jnp.float32)
    g_rows = rot_g.reshape(slots, SEQ, m_block)
    a_rows = rot_a.reshape(slots, SEQ, width)
    outer = jnp.einsum("smt,smn->stn", g_rows, a_rows, preferred_element_type=jnp.float32)
    scaled = (outer / denom[None]).astype(jnp.bfloat16)
    projected = jnp.einsum("stm,smn->stn", g_rows, scaled, preferred_element_type=jnp.float32)
    partial = jnp.sum(projected * a_rows.astype(jnp.float32), axis=2) / (dim_ff * dim_d)
    scores = lax.psum(partial, ("owner", "reader"))
    token_score = lax.dynamic_index_in_dim(scores, owner_index, 0, keepdims=False)
    slot_mean = jnp.sum(scores, axis=1) / SEQ
    table = (shuffle[:, None] == jnp.arange(slots, dtype=jnp.int32)[None, :]).astype(jnp.float32)
    example_score = jnp.sum(slot_mean[:, None] * table, axis=0)
    return (token_score, example_score)


def solution(mesh):
    return jax.shard_map(
        local,
        mesh=mesh,
        in_specs=(
            P("reader", "owner"),
            P("reader", "owner"),
            P("reader", "owner"),
            P("reader", "owner"),
            P("reader", "owner"),
            P(),
            P(),
        ),
        out_specs=(P("owner"), P()),
        check_vma=False,
    )
```

profile of v0, /device:TPU:0, one launch (start us, length us, event | category | flops | bytes accessed | tf_op | source)
XLA Modules:
  0.0 220.0 jit_solution(6955430692185103928)
XLA Ops:
  7.2 0.0 copy-start
  7.2 0.0 all-gather.3.cloned.1.call-start
  7.2 1.8 pad_maximum_fusion.1
  9.0 0.0 all-gather.3.cloned.1.call-update
  9.0 0.0 all-reduce.2.cloned.1.call-start
  9.1 57.3 %all-gather.3.cloned.1.call-done = bf16[256,9216]{1,0:T(8,128)(2,1)} async-done(((bf16[16,9216]{1,0:T(8,128)(2,1)}), bf16[256,9216]{1,0:T(8,128)(2,1)}) %all-gather.3.cloned.1.call-update) | async-done | bytes 4718608 | tf_op jit(solution)/shard_map/all_gather | solution.py:21
  66.4 0.0 copy-done
  66.4 1.7 fusion.7
  68.1 0.0 copy-start.1
  68.1 10.2 %fusion.3 = f32[256,896]{1,0:T(8,128)S(1)} fusion(bf16[896,7168]{1,0:T(8,128)(2,1)} %param.10, bf16[256,9216]{1,0:T(8,128)(2,1)} %all-gather.3.cloned.1.call-done), kind=kOutput, calls=%fused_computation.3 | convolution fusion | flops 3288334336 | bytes 17432576 | tf_op jit(solution)/shard_map/tk,jk->tj/dot_general | solution.py:24
  78.4 1.1 pad_maximum_fusion
  79.5 0.0 all-reduce.2.cloned.1.call-update
  79.5 0.0 all-gather.5.cloned.1.call-start
  79.6 0.0 copy-done.1
  79.6 0.6 fusion.10
  80.2 1.3 compare_select_fusion.1
  81.5 39.7 %all-reduce.2.cloned.1.call-done = f32[256,1152]{1,0:T(8,128)} async-done(((f32[256,1152]{1,0:T(8,128)}), f32[256,1152]{1,0:T(8,128)}) %all-reduce.2.cloned.1.call-update) | async-done | bytes 1179664 | tf_op jit(solution)/shard_map/psum | solution.py:27
  121.2 1.4 multiply_convert_fusion
  122.6 0.7 slice.22
  123.2 0.0 all-gather.5.cloned.1.call-update
  123.3 5.9 %convert_element_type.22 = f32[896,2048]{1,0:T(8,128)} convert(bf16[896,2048]{1,0:T(8,128)(2,1)} %param.11) | non-fusion elementwise | flops 1835008 | bytes 11010048 | tf_op jit(solution)/shard_map/convert_element_type | solution.py:35
  129.2 35.5 %all-gather.5.cloned.1.call-done = bf16[256,4096]{1,0:T(8,128)(2,1)} async-done(((bf16[256,256]{1,0:T(8,128)(2,1)}), bf16[256,4096]{1,0:T(8,128)(2,1)}) %all-gather.5.cloned.1.call-update) | async-done | bytes 2097168 | tf_op jit(solution)/shard_map/all_gather | solution.py:33
  164.8 1.3 constant_dynamic-slice_fusion
  166.1 0.0 copy-start.2
  166.1 6.4 %fusion.6 = f32[2,128]{1,0:T(2,128)S(1)} fusion(bf16[2,128,2048]{2,1,0:T(8,128)(2,1)S(1)} %bitcast.12, bf16[2,128,896]{2,1,0:T(8,128)(2,1)S(1)} %bitcast.13, f32[896,2048]{1,0:T(8,128)} %convert_element_type.22), kind=kOutput, calls=%fused_computation.6 | convolution fusion | flops 1887960832 | bytes 8848384 | tf_op jit(solution)/shard_map/stm,smn->stn/dot_general | solution.py:40
  172.5 39.7 %psum.15 = f32[2,128]{1,0:T(2,128)S(1)} all-reduce(f32[2,128]{1,0:T(2,128)S(1)} %broadcast_multiply_fusion), channel_id=1, replica_groups=mesh['owner'=2,'reader'=16] {'owner','reader'}, use_global_device_ids=true, to_apply=%region_2.3 | all-reduce | flops 256 | bytes 2048 | tf_op jit(solution)/shard_map/psum | solution.py:42
  212.2 0.5 dynamic-slice_bitcast_fusion
  212.7 0.1 reduce_sum.28
  212.9 0.0 copy-done.2
  212.9 0.6 fusion.9
  (4 shorter events, 0.1 us)
Async XLA Ops:
  7.2 59.3 %copy-start = (bf16[256,2048]{1,0:T(8,128)(2,1)S(1)}, bf16[256,2048]{1,0:T(8,128)(2,1)}, u32[]{:S(2)}) copy-start(bf16[256,2048]{1,0:T(8,128)(2,1)} %param.9) | copy-start | bytes 3145732
  7.2 59.2 %all-gather.3.cloned.1.call-start = ((), (), s32[]{:S(2)}) async-start(), calls=%async_computation | async-start | bytes 5013504 | tf_op jit(solution)/shard_map/all_gather | solution.py:21
  9.0 112.1 %all-reduce.2.cloned.1.call-start = ((), (), s32[]{:S(2)}) async-start(), calls=%async_computation.1 | async-start | bytes 2359296 | tf_op jit(solution)/shard_map/psum | solution.py:27
  68.1 11.5 %copy-start.1 = (s32[2]{0:T(128)S(1)}, s32[2]{0:T(128)}, u32[]{:S(2)}) copy-start(s32[2]{0:T(128)} %param.12) | copy-start | bytes 28
  79.5 85.2 %all-gather.5.cloned.1.call-start = ((), (), s32[]{:S(2)}) async-start(), calls=%async_computation.2 | async-start | bytes 2228224 | tf_op jit(solution)/shard_map/all_gather | solution.py:33
  166.1 46.8 %copy-start.2 = (s32[2]{0:T(128)S(1)}, s32[2]{0:T(128)}, u32[]{:S(2)}) copy-start(s32[2]{0:T(128)} %param.13) | copy-start | bytes 28
Sparse Core Ops, SparseCore 0:
  10.3 56.0 all-gather.2
  79.7 41.4 all-reduce.1
  123.5 41.1 all-gather.4
where the time goes:
time: 220 us
  waiting for transfers between devices  133 us (60%)
  blocking collectives  39.7 us (18%)
  matrix products  18.4 us (8%)
  between operations  13.8 us (6%)
  other arithmetic  12.3 us (6%)
  local copies, waits for them, and re-layouts  3.11 us (1%)
    all_gather x1, waiting for transfers between devices, local(): joined = lax.all_gather(joined, 'reader', axis=0, tiled=True)  57.3 us
    psum x1, blocking collectives, local(): scores = lax.psum(partial, ('owner', 'reader'))  39.7 us
    psum x1, waiting for transfers between devices, local(): whole = lax.psum(part, 'owner')  39.7 us
    all_gather x1, waiting for transfers between devices, local(): rot_a_all = lax.all_gather(rot_a_block, 'reader', axis=1, tiled=True)  35.5 us
    dot_general x1, matrix products, local(): jnp.einsum('tk,jk->tj', all_g, basis_g, preferred_element_type=jnp.float32)  10.2 us
    dot_general x1, matrix products, local(): jnp.einsum('stm,smn->stn', g_rows, scaled, preferred_element_type=jnp.flo...  6.41 us
    convert_element_type x1, other arithmetic, local(): denom = eigvals.astype(jnp.float32)  5.94 us
  transfers between devices with their start and end apart: 3, of which 3 were waited for; matrix products, arithmetic and copies ran while one was open for 4% of the time, Pallas kernels for 0%

commit v1 on v0

--- a/solution.py
+++ b/solution.py
@@ -4,6 +4,25 @@
 from jax.sharding import PartitionSpec as P
 
 SEQ = 128
+
+
+def joined_along(blocks, dim):
+    blocks = jnp.moveaxis(blocks, 0, dim)
+    lengths = blocks.shape
+    return blocks.reshape(*lengths[:dim], lengths[dim] * lengths[dim + 1], *lengths[dim + 2 :])
+
+
+def collected_by_bits(value, axis):
+    size, index = (lax.axis_size(axis), lax.axis_index(axis))
+    blocks, apart = (value[None], 1)
+    while apart < size:
+        partner_block = lax.ppermute(blocks, axis, [(i, i ^ apart) for i in range(size)])
+        low = index & apart == 0
+        blocks = jnp.concatenate(
+            [jnp.where(low, blocks, partner_block), jnp.where(low, partner_block, blocks)]
+        )
+        apart *= 2
+    return blocks
 
 
 def local(acts, grads, basis_a, basis_g, eigvals, lengths, shuffle):
@@ -18,7 +37,7 @@
     dim_ff = m_block * readers
     dim_d = width * owners
     joined = jnp.concatenate([grads, acts], axis=1)
-    joined = lax.all_gather(joined, "reader", axis=0, tiled=True)
+    joined = joined_along(collected_by_bits(joined, "reader"), 0)
     all_g = joined[:, : grads.shape[1]]
     all_a = joined[:, grads.shape[1] :]
     part_g = jnp.einsum("tk,jk->tj", all_g, basis_g, preferred_element_type=jnp.float32)

time: 220 us -> 318 us (1.45)
  waiting for transfers between devices: 133 us -> 219 us
  starting transfers between devices: 0.12 us -> 7.84 us
  other arithmetic: 12.3 us -> 18.6 us
  matrix products: 18.4 us -> 14.1 us
    ppermute x0 -> x4, waiting for transfers between devices: none -> 142 us  [collected_by_bits(): lax.ppermute(blocks, axis, [(i, i ^ apart) for i in range(size)])]
    all_gather x1 -> x0, waiting for transfers between devices: 57.3 us -> none  [local(): joined = lax.all_gather(joined, 'reader', axis=0, tiled=True)]
    ppermute x0 -> x4, starting transfers between devices: none -> 7.76 us  [collected_by_bits(): lax.ppermute(blocks, axis, [(i, i ^ apart) for i in range(size)])]
    select_n x0 -> x4, other arithmetic: none -> 4.88 us  [collected_by_bits(): jnp.where(low, blocks, partner_block)]
  transfers between devices with their start and end apart: 3 -> 6, of which waited for: 3 -> 6; matrix products, arithmetic and copies ran while one was open for 4% -> 2% of each run, Pallas kernels for 0% -> 0%
where the time goes in v1:
time: 318 us
  waiting for transfers between devices  219 us (69%)
  blocking collectives  39.7 us (12%)
  other arithmetic  18.6 us (6%)
  between operations  14.2 us (4%)
  matrix products  14.1 us (4%)
  starting transfers between devices  7.84 us (2%)
  local copies, waits for them, and re-layouts  4.05 us (1%)
    ppermute x4, waiting for transfers between devices, collected_by_bits(): lax.ppermute(blocks, axis, [(i, i ^ apart) for i in range(size)])  142 us
    psum x1, waiting for transfers between devices, local(): whole = lax.psum(part, 'owner')  41.8 us
    psum x1, blocking collectives, local(): scores = lax.psum(partial, ('owner', 'reader'))  39.7 us
    all_gather x1, waiting for transfers between devices, local(): rot_a_all = lax.all_gather(rot_a_block, 'reader', axis=1, tiled=True)  35.6 us
    ppermute x4, starting transfers between devices, collected_by_bits(): lax.ppermute(blocks, axis, [(i, i ^ apart) for i in range(size)])  7.76 us
    dot_general x1, matrix products, local(): jnp.einsum('tk,jk->tj', all_g, basis_g, preferred_element_type=jnp.float32)  7.19 us
    dot_general x1, matrix products, local(): jnp.einsum('stm,smn->stn', g_rows, scaled, preferred_element_type=jnp.flo...  6.41 us
  transfers between devices with their start and end apart: 6, of which 6 were waited for; matrix products, arithmetic and copies ran while one was open for 2% of the time, Pallas kernels for 0%

profile of v1, /device:TPU:0, one launch (start us, length us, event | category | flops | bytes accessed | tf_op | source)
XLA Modules:
  0.0 317.6 jit_solution(14576028297786686182)
XLA Ops:
  7.2 0.0 copy-start
  7.2 0.0 all-reduce.2.cloned.1.call-start
  7.2 1.1 maximum_bitcast_fusion
  8.3 0.5 collective-permute-start
  8.8 1.2 collective-permute-done
  10.0 1.1 broadcast_select_fusion.7
  11.1 0.1 pad_maximum_fusion.4
  11.2 3.0 collective-permute-start.1
  14.1 13.6 %collective-permute-done.1 = bf16[2,16,9216]{2,1,0:T(8,128)(2,1)S(1)} collective-permute-done((bf16[2,16,9216]{2,1,0:T(8,128)(2,1)S(1)}, bf16[2,16,9216]{2,1,0:T(8,128)(2,1)S(1)}, u32[]{:S(2)}, u32[]{:S(2)}) %collective-permute-start.1) | collective-permute-done | bytes 589856 | tf_op jit(solution)/shard_map/ppermute | solution.py:19
  27.8 0.1 broadcast_select_fusion.5
  27.8 0.0 copy-start.1
  27.8 0.0 copy-start.2
  27.9 0.8 copy-done.1
  28.7 0.1 pad_maximum_fusion.2
  28.8 0.1 copy-done.2
  28.9 1.8 collective-permute-start.2
  30.7 25.8 %collective-permute-done.2 = bf16[4,16,9216]{2,1,0:T(8,128)(2,1)} collective-permute-done((bf16[4,16,9216]{2,1,0:T(8,128)(2,1)S(1)}, bf16[4,16,9216]{2,1,0:T(8,128)(2,1)}, u32[]{:S(2)}, u32[]{:S(2)}) %collective-permute-start.2) | collective-permute-done | bytes 1179680 | tf_op jit(solution)/shard_map/ppermute | solution.py:19
  56.5 1.8 broadcast_select_fusion.3
  58.3 1.6 pad_maximum_fusion.1
  59.9 2.5 collective-permute-start.3
  62.4 101.2 %collective-permute-done.3 = bf16[8,16,9216]{2,1,0:T(8,128)(2,1)} collective-permute-done((bf16[8,16,9216]{2,1,0:T(8,128)(2,1)}, bf16[8,16,9216]{2,1,0:T(8,128)(2,1)}, u32[]{:S(2)}, u32[]{:S(2)}) %collective-permute-start.3) | collective-permute-done | bytes 2359328 | tf_op jit(solution)/shard_map/ppermute | solution.py:19
  163.5 2.0 broadcast_select_fusion.1
  165.5 0.4 pad_maximum_fusion
  165.9 7.2 %fusion.3 = f32[256,896]{1,0:T(8,128)S(1)} fusion(bf16[896,7168]{1,0:T(8,128)(2,1)} %param.10, bf16[256,9216]{1,0:T(8,128)(2,1)S(1)} %bitcast.19), kind=kOutput, calls=%fused_computation.4 | convolution fusion | flops 3288334336 | bytes 17432576 | tf_op jit(solution)/shard_map/tk,jk->tj/dot_general | solution.py:43
  173.1 0.0 copy-done
  173.1 0.5 fusion.7
  173.6 0.0 copy-start.3
  173.6 1.1 pad_maximum_fusion.3
  174.7 0.0 all-reduce.2.cloned.1.call-update
  174.8 0.0 all-gather.2.cloned.1.call-start
  174.8 0.0 copy-done.3
  174.8 0.6 fusion.10
  175.4 1.3 compare_select_fusion.1
  176.7 41.8 %all-reduce.2.cloned.1.call-done = f32[256,1152]{1,0:T(8,128)} async-done(((f32[256,1152]{1,0:T(8,128)}), f32[256,1152]{1,0:T(8,128)}) %all-reduce.2.cloned.1.call-update) | async-done | bytes 1179664 | tf_op jit(solution)/shard_map/psum | solution.py:46
  218.5 1.4 multiply_convert_fusion
  219.9 0.7 slice.22
  220.6 0.0 all-gather.2.cloned.1.call-update
  220.6 5.9 %convert_element_type.22 = f32[896,2048]{1,0:T(8,128)} convert(bf16[896,2048]{1,0:T(8,128)(2,1)} %param.11) | non-fusion elementwise | flops 1835008 | bytes 11010048 | tf_op jit(solution)/shard_map/convert_element_type | solution.py:54
  226.6 35.6 %all-gather.2.cloned.1.call-done = bf16[256,4096]{1,0:T(8,128)(2,1)} async-done(((bf16[256,256]{1,0:T(8,128)(2,1)}), bf16[256,4096]{1,0:T(8,128)(2,1)}) %all-gather.2.cloned.1.call-update) | async-done | bytes 2097168 | tf_op jit(solution)/shard_map/all_gather | solution.py:52
  262.1 1.3 constant_dynamic-slice_fusion
  263.4 0.0 copy-start.4
  263.4 6.4 %fusion.6 = f32[2,128]{1,0:T(2,128)S(1)} fusion(bf16[2,128,2048]{2,1,0:T(8,128)(2,1)S(1)} %bitcast.21, bf16[2,128,896]{2,1,0:T(8,128)(2,1)S(1)} %bitcast.22, f32[896,2048]{1,0:T(8,128)} %convert_element_type.22), kind=kOutput, calls=%fused_computation.10 | convolution fusion | flops 1887960832 | bytes 8848384 | tf_op jit(solution)/shard_map/stm,smn->stn/dot_general | solution.py:59
  269.9 39.7 %psum.15 = f32[2,128]{1,0:T(2,128)S(1)} all-reduce(f32[2,128]{1,0:T(2,128)S(1)} %broadcast_multiply_fusion), channel_id=1, replica_groups=mesh['owner'=2,'reader'=16] {'owner','reader'}, use_global_device_ids=true, to_apply=%region_2.3 | all-reduce | flops 256 | bytes 2048 | tf_op jit(solution)/shard_map/psum | solution.py:61
  309.6 0.5 dynamic-slice_bitcast_fusion
  310.1 0.1 reduce_sum.28
  310.2 0.0 copy-done.4
  310.2 0.6 fusion.9
  (4 shorter events, 0.1 us)
Async XLA Ops:
  7.2 166.0 %copy-start = (bf16[256,2048]{1,0:T(8,128)(2,1)S(1)}, bf16[256,2048]{1,0:T(8,128)(2,1)}, u32[]{:S(2)}) copy-start(bf16[256,2048]{1,0:T(8,128)(2,1)} %param.9) | copy-start | bytes 3145732
  7.2 211.3 %all-reduce.2.cloned.1.call-start = ((), (), s32[]{:S(2)}) async-start(), calls=%async_computation | async-start | bytes 2359296 | tf_op jit(solution)/shard_map/psum | solution.py:46
  8.3 1.7 collective-permute-start
  11.2 16.6 %collective-permute-start.1 = (bf16[2,16,9216]{2,1,0:T(8,128)(2,1)S(1)}, bf16[2,16,9216]{2,1,0:T(8,128)(2,1)S(1)}, u32[]{:S(2)}, u32[]{:S(2)}) collective-permute-start(bf16[2,16,9216]{2,1,0:T(8,128)(2,1)S(1)} %pad_maximum_fusion.4), channel_id=1, source_target_pairs={{0,2},{1,3},{2,0},{3,1},{4,6},{5,7},{6,4},{7,5},{8,10},{9,11},{10,... | collective-permute-start | bytes 1769480 | tf_op jit(solution)/shard_map/ppermute | solution.py:19
  27.8 0.8 copy-start.1
  27.8 1.0 copy-start.2
  28.9 27.6 %collective-permute-start.2 = (bf16[4,16,9216]{2,1,0:T(8,128)(2,1)S(1)}, bf16[4,16,9216]{2,1,0:T(8,128)(2,1)}, u32[]{:S(2)}, u32[]{:S(2)}) collective-permute-start(bf16[4,16,9216]{2,1,0:T(8,128)(2,1)S(1)} %pad_maximum_fusion.2), channel_id=1, source_target_pairs={{0,4},{1,5},{2,6},{3,7},{4,0},{5,1},{6,2},{7,3},{8,12},{9,13},{10,... | collective-permute-start | bytes 3538952 | tf_op jit(solution)/shard_map/ppermute | solution.py:19
  59.9 103.7 %collective-permute-start.3 = (bf16[8,16,9216]{2,1,0:T(8,128)(2,1)}, bf16[8,16,9216]{2,1,0:T(8,128)(2,1)}, u32[]{:S(2)}, u32[]{:S(2)}) collective-permute-start(bf16[8,16,9216]{2,1,0:T(8,128)(2,1)} %pad_maximum_fusion.1), channel_id=1, source_target_pairs={{0,8},{1,9},{2,10},{3,11},{4,12},{5,13},{6,14},{7,15},{8,0},{9,1},... | collective-permute-start | bytes 7077896 | tf_op jit(solution)/shard_map/ppermute | solution.py:19
  173.6 1.2 copy-start.3
  174.8 87.4 %all-gather.2.cloned.1.call-start = ((), (), s32[]{:S(2)}) async-start(), calls=%async_computation.1 | async-start | bytes 2228224 | tf_op jit(solution)/shard_map/all_gather | solution.py:52
  263.4 46.8 %copy-start.4 = (s32[2]{0:T(128)S(1)}, s32[2]{0:T(128)}, u32[]{:S(2)}) copy-start(s32[2]{0:T(128)} %param.13) | copy-start | bytes 28
Sparse Core Ops, SparseCore 0:
  174.9 43.5 all-reduce.1
  220.9 41.1 all-gather.1

commit v2 on v0

--- a/solution.py
+++ b/solution.py
@@ -4,6 +4,12 @@
 from jax.sharding import PartitionSpec as P
 
 SEQ = 128
+
+
+def gather_and_add(x, name):
+    parts = lax.all_gather(x, name, axis=0, tiled=False)
+    total = parts.sum(axis=0)
+    return total
 
 
 def local(acts, grads, basis_a, basis_g, eigvals, lengths, shuffle):
@@ -24,7 +30,7 @@
     part_g = jnp.einsum("tk,jk->tj", all_g, basis_g, preferred_element_type=jnp.float32)
     part_a = jnp.einsum("tk,jk->tj", all_a, basis_a, preferred_element_type=jnp.float32)
     part = jnp.concatenate([part_g, part_a], axis=1)
-    whole = lax.psum(part, "owner")
+    whole = gather_and_add(part, "owner")
     token = jnp.arange(rows, dtype=jnp.int32)
     live = (token % SEQ < lengths[token // SEQ]).astype(jnp.float32)
     rot = (whole * live[:, None]).astype(jnp.bfloat16)

time: 220 us -> 214 us (0.973)
  waiting for transfers between devices: 133 us -> 126 us
    psum x1 -> x0, waiting for transfers between devices: 39.7 us -> none  [local(): whole = lax.psum(part, 'owner')]
    all_gather x0 -> x1, waiting for transfers between devices: none -> 32.8 us  [gather_and_add(): parts = lax.all_gather(x, name, axis=0, tiled=False)]
where the time goes in v2:
time: 214 us
  waiting for transfers between devices  126 us (59%)
  blocking collectives  39.7 us (19%)
  matrix products  18.4 us (9%)
  between operations  13.8 us (6%)
  other arithmetic  12.9 us (6%)
  local copies, waits for them, and re-layouts  3.11 us (1%)
    all_gather x1, waiting for transfers between devices, local(): joined = lax.all_gather(joined, 'reader', axis=0, tiled=True)  57.3 us
    psum x1, blocking collectives, local(): scores = lax.psum(partial, ('owner', 'reader'))  39.7 us
    all_gather x1, waiting for transfers between devices, local(): rot_a_all = lax.all_gather(rot_a_block, 'reader', axis=1, tiled=True)  35.4 us
    all_gather x1, waiting for transfers between devices, gather_and_add(): parts = lax.all_gather(x, name, axis=0, tiled=False)  32.8 us
    dot_general x1, matrix products, local(): jnp.einsum('tk,jk->tj', all_g, basis_g, preferred_element_type=jnp.float32)  10.2 us
    dot_general x1, matrix products, local(): jnp.einsum('stm,smn->stn', g_rows, scaled, preferred_element_type=jnp.flo...  6.41 us
    convert_element_type x1, other arithmetic, local(): denom = eigvals.astype(jnp.float32)  5.94 us
  transfers between devices with their start and end apart: 3, of which 3 were waited for; matrix products, arithmetic and copies ran while one was open for 4% of the time, Pallas kernels for 0%

profile of v2, /device:TPU:0, one launch (start us, length us, event | category | flops | bytes accessed | tf_op | source)
XLA Modules:
  0.0 213.6 jit_solution(15283375836024627101)
XLA Ops:
  7.2 0.0 copy-start
  7.2 0.0 all-gather.5.cloned.1.call-start
  7.2 1.8 pad_maximum_fusion.1
  9.0 0.0 all-gather.5.cloned.1.call-update
  9.0 0.0 all-gather.9.cloned.1.call-start
  9.1 57.3 %all-gather.5.cloned.1.call-done = bf16[256,9216]{1,0:T(8,128)(2,1)} async-done(((bf16[16,9216]{1,0:T(8,128)(2,1)}), bf16[256,9216]{1,0:T(8,128)(2,1)}) %all-gather.5.cloned.1.call-update) | async-done | bytes 4718608 | tf_op jit(solution)/shard_map/all_gather | solution.py:27
  66.4 0.0 copy-done
  66.4 1.7 fusion.7
  68.1 0.0 copy-start.1
  68.1 10.2 %fusion.3 = f32[256,896]{1,0:T(8,128)S(1)} fusion(bf16[896,7168]{1,0:T(8,128)(2,1)} %param.10, bf16[256,9216]{1,0:T(8,128)(2,1)} %all-gather.5.cloned.1.call-done), kind=kOutput, calls=%fused_computation.3 | convolution fusion | flops 3288334336 | bytes 17432576 | tf_op jit(solution)/shard_map/tk,jk->tj/dot_general | solution.py:30
  78.4 1.1 pad_maximum_fusion
  79.5 0.0 all-gather.9.cloned.1.call-update
  79.5 0.0 all-gather.7.cloned.1.call-start
  79.6 0.0 copy-done.1
  79.6 0.6 fusion.10
  80.2 1.3 compare_select_fusion.1
  81.5 32.8 %all-gather.9.cloned.1.call-done = f32[512,1152]{1,0:T(8,128)} async-done(((f32[256,1152]{1,0:T(8,128)}), f32[512,1152]{1,0:T(8,128)}) %all-gather.9.cloned.1.call-update) | async-done | bytes 2359312 | tf_op jit(solution)/shard_map/all_gather | solution.py:10
  114.3 1.9 reduce_sum.36
  116.2 0.1 multiply_convert_fusion
  116.4 0.7 slice.22
  117.0 0.0 all-gather.7.cloned.1.call-update
  117.1 5.9 %convert_element_type.22 = f32[896,2048]{1,0:T(8,128)} convert(bf16[896,2048]{1,0:T(8,128)(2,1)} %param.11) | non-fusion elementwise | flops 1835008 | bytes 11010048 | tf_op jit(solution)/shard_map/convert_element_type | solution.py:41
  123.0 35.4 %all-gather.7.cloned.1.call-done = bf16[256,4096]{1,0:T(8,128)(2,1)} async-done(((bf16[256,256]{1,0:T(8,128)(2,1)}), bf16[256,4096]{1,0:T(8,128)(2,1)}) %all-gather.7.cloned.1.call-update) | async-done | bytes 2097168 | tf_op jit(solution)/shard_map/all_gather | solution.py:39
  158.4 1.3 constant_dynamic-slice_fusion
  159.7 0.0 copy-start.2
  159.7 6.4 %fusion.6 = f32[2,128]{1,0:T(2,128)S(1)} fusion(bf16[2,128,2048]{2,1,0:T(8,128)(2,1)S(1)} %bitcast.14, bf16[2,128,896]{2,1,0:T(8,128)(2,1)S(1)} %bitcast.15, f32[896,2048]{1,0:T(8,128)} %convert_element_type.22), kind=kOutput, calls=%fused_computation.6 | convolution fusion | flops 1887960832 | bytes 8848384 | tf_op jit(solution)/shard_map/stm,smn->stn/dot_general | solution.py:46
  166.1 39.7 %psum.7 = f32[2,128]{1,0:T(2,128)S(1)} all-reduce(f32[2,128]{1,0:T(2,128)S(1)} %broadcast_multiply_fusion), channel_id=1, replica_groups=mesh['owner'=2,'reader'=16] {'owner','reader'}, use_global_device_ids=true, to_apply=%region_2.3 | all-reduce | flops 256 | bytes 2048 | tf_op jit(solution)/shard_map/psum | solution.py:48
  205.8 0.1 reduce_sum.38
  206.0 0.5 dynamic-slice_bitcast_fusion
  206.5 0.0 copy-done.2
  206.5 0.6 fusion.9
  (4 shorter events, 0.1 us)
Async XLA Ops:
  7.2 59.3 %copy-start = (bf16[256,2048]{1,0:T(8,128)(2,1)S(1)}, bf16[256,2048]{1,0:T(8,128)(2,1)}, u32[]{:S(2)}) copy-start(bf16[256,2048]{1,0:T(8,128)(2,1)} %param.9) | copy-start | bytes 3145732
  7.2 59.2 %all-gather.5.cloned.1.call-start = ((), (), s32[]{:S(2)}) async-start(), calls=%async_computation | async-start | bytes 5013504 | tf_op jit(solution)/shard_map/all_gather | solution.py:27
  9.0 105.3 %all-gather.9.cloned.1.call-start = ((), (), s32[]{:S(2)}) async-start(), calls=%async_computation.2 | async-start | bytes 3538944 | tf_op jit(solution)/shard_map/all_gather | solution.py:10
  68.1 11.4 %copy-start.1 = (s32[2]{0:T(128)S(1)}, s32[2]{0:T(128)}, u32[]{:S(2)}) copy-start(s32[2]{0:T(128)} %param.12) | copy-start | bytes 28
  79.5 78.9 %all-gather.7.cloned.1.call-start = ((), (), s32[]{:S(2)}) async-start(), calls=%async_computation.1 | async-start | bytes 2228224 | tf_op jit(solution)/shard_map/all_gather | solution.py:39
  159.7 46.8 %copy-start.2 = (s32[2]{0:T(128)S(1)}, s32[2]{0:T(128)}, u32[]{:S(2)}) copy-start(s32[2]{0:T(128)} %param.13) | copy-start | bytes 28
Sparse Core Ops, SparseCore 0:
  10.3 56.0 all-gather.4
  79.6 34.6 all-gather.8
  117.2 41.1 all-gather.6
